TPU v7x, 512 devices: a whole 4x4x16 slice. The times are simulated.
512 devices in a mesh: ctx: 32 (over y_hi, z), fsdp: 16 (over y_lo, x, core).
Axes of the slice: x: 4, y: 4 (y_hi: 2, y_lo: 2; y = y_hi * 2 + y_lo), z: 16, core: 2. Of those that a mesh axis runs over, the one named last changes fastest.
Arguments:
- latents: bfloat16 [10240, 3072], P('ctx'), may hold values from -6 to 6, as said below
- timestep: int32 [1], replicated, may hold values from 0 to 999
- offsets: int32 [64], replicated, may hold values from 0 to 63, as said below
- qkv_weight: bfloat16 [3072, 16, 384], P('ctx', 'fsdp'), may hold values from -2 to 2
- mod_weight: bfloat16 [3072, 2, 256], P('ctx'), may hold values from -0.375 to 0.375
- gate_weight: bfloat16 [256, 3072], P(None, 'fsdp'), may hold values from -0.375 to 0.375
- out_weight: bfloat16 [3072, 16, 128], P('ctx', 'fsdp'), may hold values from -0.125 to 0.125
- conv_weight: bfloat16 [3, 3, 3, 3072], P(None, None, None, 'fsdp'), may hold values from -1.25 to 1.25
Outputs:
- mixed: bfloat16 [10240, 3072], P('ctx', 'fsdp')
Inputs may be any that keep to these rules, and one draw needn't show every extreme that they name: `latents`: tokens in order of frame, then row, then column. offsets[f] is at most f; the last frame's offset is exactly 63.
All inputs are finite; a program needn't handle non-finite values.
Results may differ from a plain program's by a relative error of at most 0.0095.
Values may be sent and summed in bfloat16 or wider, within the bound.
No kernel may reach another device: no remote copies, remote signals or barrier semaphores. Data moves between devices by JAX's collectives and lax.ppermute only.
A program may use at most 64 MiB of HBM per device.

v0:
```python
import math
import jax
import jax.numpy as jnp
from jax import lax
from jax.sharding import PartitionSpec as P

HH = 10
WW = 16
EPS = 1e-06
NEG = -1e30


def passed_along(block, axis, distance):
    devices = range(lax.axis_size(axis))
    route = [(i - distance, i) for i in devices if i - distance in devices]
    return lax.ppermute(block, axis, route)


def time_features(timestep, embed_width):
    half_width = embed_width // 2
    freqs = jnp.exp(-math.log(10000.0) * jnp.arange(half_width, dtype=jnp.float32) / half_width)
    angles = timestep[0].astype(jnp.float32) * freqs
    embed = jnp.concatenate([jnp.cos(angles), jnp.sin(angles)])
    return jax.nn.silu(embed).astype(jnp.bfloat16)


def attend_piece(
    state_now, kv_piece, first_key, queries, query_frame, query_first, frame_size, head_dim
):
    run_max, run_sum, accumulated = state_now
    key_count = kv_piece.shape[0]
    key_part = kv_piece[:, :, :head_dim]
    value_part = kv_piece[:, :, head_dim:]
    scores = jnp.einsum(
        "nhe,mhe->nhm", queries, key_part, preferred_element_type=jnp.float32
    ) * head_dim ** (-0.5)
    key_frame = (first_key + jnp.arange(key_count, dtype=jnp.int32)) // frame_size
    allowed = (key_frame[None, :] <= query_frame[:, None]) & (
        key_frame[None, :] >= query_first[:, None]
    )
    masked = jnp.where(allowed[:, None, :], scores, NEG)
    new_max = jnp.maximum(run_max, masked.max(-1))
    exponent = jnp.where(allowed[:, None, :], jnp.exp(masked - new_max[..., None]), 0.0)
    factor = jnp.exp(run_max - new_max)
    run_sum = run_sum * factor + exponent.sum(-1)
    accumulated = accumulated * factor[..., None] + jnp.einsum(
        "nhm,mhe->nhe",
        exponent.astype(jnp.bfloat16),
        value_part,
        preferred_element_type=jnp.float32,
    )
    return (new_max, run_sum, accumulated)


def fold_blocks(state_now, kv_piece, step_fn, block_rows):
    key_count = kv_piece.shape[0]
    split_rows = kv_piece.reshape(
        key_count // block_rows, block_rows, kv_piece.shape[1], kv_piece.shape[2]
    )

    def visit_block(state_in, block_item):
        block_no, block_rows_kv = block_item
        return (step_fn(state_in, block_rows_kv, block_no * block_rows), None)

    block_ids = jnp.arange(key_count // block_rows, dtype=jnp.int32)
    state_out, _ = lax.scan(visit_block, state_now, (block_ids, split_rows))
    return state_out


def per_device(
    latents, timestep, offsets, qkv_weight, mod_weight, gate_weight, out_weight, conv_weight
):
    tok_rows = latents.shape[0]
    heads_here = qkv_weight.shape[1]
    head_dim = out_weight.shape[2]
    chan_here = gate_weight.shape[1]
    frame_size = HH * WW
    frames_here = tok_rows // frame_size
    position = lax.axis_index("ctx")
    column = lax.axis_index("fsdp")
    time_act = time_features(timestep, gate_weight.shape[0])
    gate_vec = jnp.dot(time_act, gate_weight, preferred_element_type=jnp.float32)
    float_rows = latents.astype(jnp.float32)
    centred = float_rows - float_rows.mean(-1, keepdims=True)
    variance = (centred * centred).mean(-1, keepdims=True)
    normed = centred * lax.rsqrt(variance + EPS)
    rows_here = qkv_weight.shape[0]
    qkv_width = qkv_weight.shape[2]
    local_shares = jnp.einsum("rjt,t->rj", mod_weight, time_act, preferred_element_type=jnp.float32)
    shares_hi = local_shares.astype(jnp.bfloat16)
    shares_lo = (local_shares - shares_hi.astype(jnp.float32)).astype(jnp.bfloat16)
    bundle = jnp.concatenate(
        [
            qkv_weight.reshape(rows_here, heads_here * qkv_width),
            out_weight.reshape(rows_here, heads_here * head_dim),
            shares_hi,
            shares_lo,
        ],
        axis=1,
    )
    gathered = lax.all_gather(bundle, "ctx", axis=0, tiled=True)
    full_rows = gathered.shape[0]
    qkv_cols = heads_here * qkv_width
    out_cols = heads_here * head_dim
    w_piece = gathered[:, :qkv_cols].reshape(full_rows, heads_here, qkv_width)
    o_piece = gathered[:, qkv_cols : qkv_cols + out_cols].reshape(full_rows, heads_here, head_dim)
    share_bits = gathered[:, qkv_cols + out_cols :].astype(jnp.float32)
    shares = share_bits[:, :2] + share_bits[:, 2:]
    modulated = (normed * (1.0 + shares[:, 1]) + shares[:, 0]).astype(jnp.bfloat16)
    projected_qkv = jnp.einsum(
        "nr,rhc->nhc", modulated, w_piece, preferred_element_type=jnp.float32
    ).astype(jnp.bfloat16)
    queries = projected_qkv[:, :, :head_dim]
    packed = projected_qkv[:, :, head_dim:]
    query_frame = position * frames_here + jnp.arange(tok_rows, dtype=jnp.int32) // frame_size
    local_first = lax.dynamic_slice_in_dim(offsets, position * frames_here, frames_here, 0)
    query_first = jnp.repeat(local_first, frame_size)
    start_state = (
        jnp.full((tok_rows, heads_here), NEG, jnp.float32),
        jnp.zeros((tok_rows, heads_here), jnp.float32),
        jnp.zeros((tok_rows, heads_here, head_dim), jnp.float32),
    )
    block_rows = 2 * tok_rows

    def attend(state_now, kv_piece, first_key):
        return attend_piece(
            state_now, kv_piece, first_key, queries, query_frame, query_first, frame_size, head_dim
        )

    run_max, run_sum, accumulated = fold_blocks(
        start_state, lax.all_gather(packed, "ctx", axis=0, tiled=True), attend, block_rows
    )
    attended = (accumulated / run_sum[..., None]).astype(jnp.bfloat16)
    partial_out = jnp.einsum("nhe,rhe->nr", attended, o_piece, preferred_element_type=jnp.float32)
    head_total = lax.psum_scatter(
        partial_out.astype(jnp.bfloat16), "fsdp", scatter_dimension=1, tiled=True
    ).astype(jnp.float32)
    own_chan = lax.dynamic_slice_in_dim(latents, column * chan_here, chan_here, 1)
    before = passed_along(own_chan, "ctx", 1)
    stacked = (
        jnp.concatenate([before, own_chan], 0)
        .astype(jnp.float32)
        .reshape(frames_here + 2, HH, WW, chan_here)
    )
    padded = jnp.pad(stacked, ((0, 0), (1, 1), (1, 1), (0, 0)))
    convolved = jnp.zeros((frames_here, HH, WW, chan_here), jnp.float32)
    for time_lag in range(3):
        for row_shift in range(3):
            for col_shift in range(3):
                tap = conv_weight[time_lag, row_shift, col_shift].astype(jnp.float32)
                convolved = (
                    convolved
                    + tap
                    * padded[
                        2 - time_lag : 2 - time_lag + frames_here,
                        row_shift : row_shift + HH,
                        col_shift : col_shift + WW,
                    ]
                )
    residual = own_chan.astype(jnp.float32)
    mixed = residual + gate_vec * head_total + convolved.reshape(tok_rows, chan_here)
    return mixed.astype(jnp.bfloat16)


def solution(mesh):
    in_specs = (
        P("ctx", None),
        P(),
        P(),
        P("ctx", "fsdp", None),
        P("ctx", None, None),
        P(None, "fsdp"),
        P("ctx", "fsdp", None),
        P(None, None, None, "fsdp"),
    )
    out_specs = P("ctx", "fsdp")
    return jax.shard_map(
        per_device, mesh=mesh, in_specs=in_specs, out_specs=out_specs, check_vma=False
    )
```

profile of v0, /device:TPU:32, one launch (start us, length us, event | category | flops | bytes accessed | tf_op | source)
XLA Modules:
  0.0 485.3 jit_solution(17367744901689047)
XLA Ops:
  7.9 1.6 pad_maximum_fusion
  9.6 1.9 convert_reduce_fusion
  11.5 0.7 fusion.28
  12.2 165.2 %all-gather.3.cloned.1.call-done = bf16[3072,516]{1,0:T(8,128)(2,1)} async-done(((bf16[96,516]{1,0:T(8,128)(2,1)}), bf16[3072,516]{1,0:T(8,128)(2,1)}) %all-gather.3.cloned.1.call-update) | async-done | bytes 3170320 | tf_op jit(solution)/shard_map/all_gather | solution.py:101
  177.3 1.2 slice_convert_fusion
  178.6 0.5 slice_add_fusion.1
  179.1 1.3 fusion.39
  180.7 1.3 fusion.45
  181.9 0.7 slice.289
  182.8 166.0 %all-gather.5.cloned.1.call-done = bf16[10240,1,256]{2,0,1:T(8,128)(2,1)} async-done(((bf16[320,1,256]{2,0,1:T(8,128)(2,1)}), bf16[10240,1,256]{2,0,1:T(8,128)(2,1)}) %all-gather.5.cloned.1.call-update) | async-done | bytes 5242896 | tf_op jit(solution)/shard_map/all_gather | solution.py:131
  348.9 58.9 %while.17 = (s32[]{:T(128)}, f32[320,1]{0,1:T(1,128)S(1)}, f32[320,1]{0,1:T(1,128)S(1)}, f32[320,1,128]{2,0,1:T(8,128)S(1)}, s32[16]{0:T(128)S(1)}, /*index=5*/b...) while((s32[]{:T(128)}, f32[320,1]{0,1:T(1,128)S(1)}, ...), condition=%wide.region_5.6_spmd.clone, body=%wide.region_2.5_spmd.clone.sunk | while | flops 108677440 | bytes 3902893 | solution.py:66
  348.9 0.6 dynamic_slice.29
  350.0 1.0 dynamic-slice_bitcast_fusion.2
  351.2 0.4 fusion.122
  352.5 0.6 dynamic_slice.29
  353.7 1.0 dynamic-slice_bitcast_fusion.2
  354.9 0.4 fusion.122
  356.2 0.6 dynamic_slice.29
  357.4 1.0 dynamic-slice_bitcast_fusion.2
  358.6 0.4 fusion.122
  359.9 0.6 dynamic_slice.29
  361.1 1.0 dynamic-slice_bitcast_fusion.2
  362.3 0.4 fusion.122
  363.6 0.6 dynamic_slice.29
  364.8 1.0 dynamic-slice_bitcast_fusion.2
  366.0 0.4 fusion.122
  367.3 0.6 dynamic_slice.29
  368.5 1.0 dynamic-slice_bitcast_fusion.2
  369.6 0.4 fusion.122
  371.0 0.6 dynamic_slice.29
  372.1 1.0 dynamic-slice_bitcast_fusion.2
  373.3 0.4 fusion.122
  374.6 0.6 dynamic_slice.29
  375.8 1.0 dynamic-slice_bitcast_fusion.2
  377.0 0.4 fusion.122
  378.3 0.6 dynamic_slice.29
  379.5 1.0 dynamic-slice_bitcast_fusion.2
  380.7 0.4 fusion.122
  382.0 0.6 dynamic_slice.29
  383.2 1.0 dynamic-slice_bitcast_fusion.2
  384.4 0.4 fusion.122
  385.7 0.6 dynamic_slice.29
  386.9 1.0 dynamic-slice_bitcast_fusion.2
  388.0 0.4 fusion.122
  389.4 0.6 dynamic_slice.29
  390.5 1.0 dynamic-slice_bitcast_fusion.2
  391.7 0.4 fusion.122
  393.0 0.6 dynamic_slice.29
  394.2 1.0 dynamic-slice_bitcast_fusion.2
  396.7 0.6 dynamic_slice.29
  397.9 1.0 dynamic-slice_bitcast_fusion.2
  399.1 0.4 fusion.122
  400.4 0.6 dynamic_slice.29
  401.6 1.0 dynamic-slice_bitcast_fusion.2
  402.8 0.4 fusion.122
  404.1 0.6 dynamic_slice.29
  405.3 1.0 dynamic-slice_bitcast_fusion.2
  406.4 0.4 fusion.122
  407.8 3.4 convolution_convert_fusion
  411.5 2.3 collective-permute-start
  414.0 4.5 collective-permute-done
  419.6 0.8 fusion.96
  420.5 56.5 %reduce-scatter.2.cloned.1.call-done = bf16[320,192]{0,1:T(8,128)(2,1)} async-done(((bf16[320,3072]{0,1:T(8,128)(2,1)}), bf16[320,192]{0,1:T(8,128)(2,1)}) %reduce-scatter.2.cloned.1.call-update) | async-done | bytes 122896 | tf_op jit(solution)/shard_map/reduce_scatter | solution.py:135
  477.0 1.7 add_convert_fusion
  (192 shorter events, 19.4 us)
Async XLA Ops:
  6.5 0.9 copy-start
  6.5 5.0 %copy-start.1 = (bf16[320,3072]{1,0:T(8,128)(2,1)S(1)}, bf16[320,3072]{1,0:T(8,128)(2,1)}, u32[]{:S(2)}) copy-start(bf16[320,3072]{1,0:T(8,128)(2,1)} %param.10) | copy-start | bytes 5898244
  6.5 170.8 %all-gather.3.cloned.1.call-start = ((), (), s32[]{:S(2)}) async-start(), calls=%async_computation.1 | async-start | bytes 4055040 | tf_op jit(solution)/shard_map/all_gather | solution.py:101
  9.5 339.3 %all-gather.5.cloned.1.call-start = ((), (), s32[]{:S(2)}) async-start(), calls=%async_computation.2 | async-start | bytes 5406720 | tf_op jit(solution)/shard_map/all_gather | solution.py:131
  178.6 2.1 copy-start.2
  180.7 2.1 copy-start.5
  182.7 294.4 %reduce-scatter.2.cloned.1.call-start = ((), (), s32[]{:S(2)}) async-start(), calls=%async_computation.3 | async-start | bytes 2506752 | tf_op jit(solution)/shard_map/reduce_scatter | solution.py:135
  411.2 2.7 copy-start.4
  411.2 2.7 copy-start.3
  411.5 7.0 %collective-permute-start = (bf16[320,192]{0,1:T(8,128)(2,1)S(1)}, bf16[320,192]{0,1:T(8,128)(2,1)S(1)}, u32[]{:S(2)}, u32[]{:S(2)}) collective-permute-start(bf16[320,192]{0,1:T(8,128)(2,1)S(1)} %copy.30), channel_id=1, source_target_pairs={{0,16},{16,32},{32,48},{48,64},{64,80},{80,96},{96,112},{112,128},... | collective-permute-start | bytes 368648 | tf_op jit(solution)/shard_map/ppermute | solution.py:16
Sparse Core Ops, SparseCore 0:
  10.5 166.8 all-gather.2
  182.8 166.0 all-gather.4
  411.3 65.6 reduce-scatter.1
where the time goes:
time: 487 us; the launch traced here: 485 us
  waiting for transfers between devices  392 us (80%)
  local copies, waits for them, and re-layouts  30.7 us (6%)
  matrix products  18.5 us (4%)
  other arithmetic  17.3 us (4%)
  between operations  14.2 us (3%)
  loops' own time  10 us (2%)
    all_gather x1, waiting for transfers between devices, per_device(): lax.all_gather(packed, 'ctx', axis=0, tiled=True)  166 us
    all_gather x1, waiting for transfers between devices, per_device(): gathered = lax.all_gather(bundle, 'ctx', axis=0, tiled=True)  165 us
    reduce_scatter x1, waiting for transfers between devices, per_device(): lax.psum_scatter(partial_out.astype(jnp.bfloat16), 'fsdp', scatter_dimens...  56.5 us
    squeeze x16, local copies, waits for them, and re-layouts, fold_blocks(): state_out, _ = lax.scan(visit_block, state_now, (block_ids, split_rows))  16 us
    another operation x1, loops' own time, fold_blocks(): state_out, _ = lax.scan(visit_block, state_now, (block_ids, split_rows))  10 us
  transfers between devices with their start and end apart: 4, of which 4 were waited for; matrix products, arithmetic and copies ran while one was open for 1% of the time, Pallas kernels for 0%

commit v1 on v0

--- a/solution.py
+++ b/solution.py
@@ -128,7 +128,12 @@
         )
 
     run_max, run_sum, accumulated = fold_blocks(
-        start_state, lax.all_gather(packed, "ctx", axis=0, tiled=True), attend, block_rows
+        start_state,
+        jnp.concatenate(
+            lax.all_to_all(jnp.stack([packed] * lax.axis_size("ctx")), "ctx", 0, 0), axis=0
+        ),
+        attend,
+        block_rows,
     )
     attended = (accumulated / run_sum[..., None]).astype(jnp.bfloat16)
     partial_out = jnp.einsum("nhe,rhe->nr", attended, o_piece, preferred_element_type=jnp.float32)

time: 487 us -> 556 us (1.14)
  the two profiles are of different devices: /device:TPU:32 before, /device:TPU:16 now
where the time goes in v1:
time: 556 us; the launch traced here: 555 us
  waiting for transfers between devices  442 us (79%)
  local copies, waits for them, and re-layouts  33.3 us (6%)
  starting transfers between devices  18.8 us (3%)
  matrix products  18.5 us (3%)
  other arithmetic  17.3 us (3%)
  between operations  14.5 us (3%)
  loops' own time  11 us (2%)
    all_to_all x1, waiting for transfers between devices, per_device(): lax.all_to_all(jnp.stack([packed] * lax.axis_size('ctx')), 'ctx', 0, 0)  220 us
    all_gather x1, waiting for transfers between devices, per_device(): gathered = lax.all_gather(bundle, 'ctx', axis=0, tiled=True)  162 us
    reduce_scatter x1, waiting for transfers between devices, per_device(): lax.psum_scatter(partial_out.astype(jnp.bfloat16), 'fsdp', scatter_dimens...  57.3 us
    squeeze x16, local copies, waits for them, and re-layouts, fold_blocks(): state_out, _ = lax.scan(visit_block, state_now, (block_ids, split_rows))  16 us
  transfers between devices with their start and end apart: 4, of which 4 were waited for; matrix products, arithmetic and copies ran while one was open for 1% of the time, Pallas kernels for 0%

profile of v1, /device:TPU:16, one launch (start us, length us, event | category | flops | bytes accessed | tf_op | source)
XLA Modules:
  0.0 555.1 jit_solution(15145927185033398160)
XLA Ops:
  7.9 1.6 pad_maximum_fusion
  9.5 1.9 convert_reduce_fusion
  11.4 0.7 fusion.28
  12.1 162.4 %all-gather.2.cloned.1.call-done = bf16[3072,516]{1,0:T(8,128)(2,1)} async-done(((bf16[96,516]{1,0:T(8,128)(2,1)}), bf16[3072,516]{1,0:T(8,128)(2,1)}) %all-gather.2.cloned.1.call-update) | async-done | bytes 3170320 | tf_op jit(solution)/shard_map/all_gather | solution.py:101
  174.6 1.2 slice_convert_fusion
  175.8 0.5 slice_add_fusion.1
  176.3 1.3 fusion.39
  177.9 1.3 fusion.45
  179.2 2.9 stack.2
  182.1 10.8 %all-to-all-start = ((bf16[32,320,1,256]{3,1,2,0:T(8,128)(2,1)}), bf16[32,320,1,256]{3,1,2,0:T(8,128)(2,1)}, u32[]{:S(2)}, u32[]{:S(2)}) async-start(bf16[32,320,1,256]{3,1,2,0:T(8,128)(2,1)} %stack.2), calls=%async_computation | async-start | bytes 10485760 | tf_op jit(solution)/shard_map/all_to_all | solution.py:133
  193.2 219.5 %all-to-all-done = bf16[32,320,1,256]{3,1,2,0:T(8,128)(2,1)} async-done(((bf16[32,320,1,256]{3,1,2,0:T(8,128)(2,1)}), bf16[32,320,1,256]{3,1,2,0:T(8,128)(2,1)}, u32[]{:S(2)}, u32[]{:S(2)}) %all-to-all-start) | async-done | bytes 5242912 | tf_op jit(solution)/shard_map/all_to_all | solution.py:133
  412.7 60.2 %while.17 = (s32[]{:T(128)}, f32[320,1]{0,1:T(1,128)S(1)}, f32[320,1]{0,1:T(1,128)S(1)}, f32[320,1,128]{2,0,1:T(8,128)S(1)}, s32[16]{0:T(128)S(1)}, /*index=5*/b...) while((s32[]{:T(128)}, f32[320,1]{0,1:T(1,128)S(1)}, ...), condition=%wide.region_5.6_spmd.clone, body=%wide.region_2.5_spmd.clone.sunk | while | flops 108677440 | bytes 3902893 | solution.py:66
  412.7 0.6 dynamic_slice.29
  414.0 1.0 dynamic-slice_bitcast_fusion.2
  415.1 0.4 fusion.122
  416.5 0.6 dynamic_slice.29
  417.7 1.0 dynamic-slice_bitcast_fusion.2
  418.9 0.4 fusion.122
  420.2 0.6 dynamic_slice.29
  421.5 1.0 dynamic-slice_bitcast_fusion.2
  422.7 0.4 fusion.122
  424.0 0.6 dynamic_slice.29
  425.3 1.0 dynamic-slice_bitcast_fusion.2
  426.4 0.4 fusion.122
  427.7 0.6 dynamic_slice.29
  429.0 1.0 dynamic-slice_bitcast_fusion.2
  430.2 0.4 fusion.122
  431.5 0.6 dynamic_slice.29
  432.8 1.0 dynamic-slice_bitcast_fusion.2
  433.9 0.4 fusion.122
  435.3 0.6 dynamic_slice.29
  436.5 1.0 dynamic-slice_bitcast_fusion.2
  437.7 0.4 fusion.122
  439.0 0.6 dynamic_slice.29
  440.3 1.0 dynamic-slice_bitcast_fusion.2
  441.5 0.4 fusion.122
  442.8 0.6 dynamic_slice.29
  444.1 1.0 dynamic-slice_bitcast_fusion.2
  445.2 0.4 fusion.122
  446.6 0.6 dynamic_slice.29
  447.8 1.0 dynamic-slice_bitcast_fusion.2
  449.0 0.4 fusion.122
  450.3 0.6 dynamic_slice.29
  451.6 1.0 dynamic-slice_bitcast_fusion.2
  452.8 0.4 fusion.122
  454.1 0.6 dynamic_slice.29
  455.3 1.0 dynamic-slice_bitcast_fusion.2
  456.5 0.4 fusion.122
  457.8 0.6 dynamic_slice.29
  459.1 1.0 dynamic-slice_bitcast_fusion.2
  461.6 0.6 dynamic_slice.29
  462.9 1.0 dynamic-slice_bitcast_fusion.2
  464.0 0.4 fusion.122
  465.4 0.6 dynamic_slice.29
  466.6 1.0 dynamic-slice_bitcast_fusion.2
  469.1 0.6 dynamic_slice.29
  470.4 1.0 dynamic-slice_bitcast_fusion.2
  471.6 0.4 fusion.122
  472.9 3.4 convolution_convert_fusion
  476.6 8.0 %collective-permute-start = (bf16[320,192]{0,1:T(8,128)(2,1)S(1)}, bf16[320,192]{0,1:T(8,128)(2,1)S(1)}, u32[]{:S(2)}, u32[]{:S(2)}) collective-permute-start(bf16[320,192]{0,1:T(8,128)(2,1)S(1)} %copy.36), channel_id=1, source_target_pairs={{0,16},{16,32},{32,48},{48,64},{64,80},{80,96},{96,112},{112,128},... | collective-permute-start | bytes 368648 | tf_op jit(solution)/shard_map/ppermute | solution.py:16
  484.8 2.4 collective-permute-done
  488.3 0.8 fusion.96
  489.3 57.3 %reduce-scatter.2.cloned.1.call-done = bf16[320,192]{0,1:T(8,128)(2,1)} async-done(((bf16[320,3072]{0,1:T(8,128)(2,1)}), bf16[320,192]{0,1:T(8,128)(2,1)}) %reduce-scatter.2.cloned.1.call-update) | async-done | bytes 122896 | tf_op jit(solution)/shard_map/reduce_scatter | solution.py:140
  546.6 1.7 add_convert_fusion
  (192 shorter events, 19.8 us)
Async XLA Ops:
  6.5 0.9 copy-start
  6.5 4.9 copy-start.1
  6.5 168.0 %all-gather.2.cloned.1.call-start = ((), (), s32[]{:S(2)}) async-start(), calls=%async_computation.2 | async-start | bytes 4055040 | tf_op jit(solution)/shard_map/all_gather | solution.py:101
  175.8 2.1 copy-start.2
  182.1 10.9 %copy-start.5 = (s32[64]{0:T(128)S(1)}, s32[64]{0:T(128)}, u32[]{:S(2)}) copy-start(s32[64]{0:T(128)} %param.12) | copy-start | bytes 772
  182.1 230.6 %all-to-all-start = ((bf16[32,320,1,256]{3,1,2,0:T(8,128)(2,1)}), bf16[32,320,1,256]{3,1,2,0:T(8,128)(2,1)}, u32[]{:S(2)}, u32[]{:S(2)}) async-start(bf16[32,320,1,256]{3,1,2,0:T(8,128)(2,1)} %stack.2), calls=%async_computation | async-start | bytes 10485760 | tf_op jit(solution)/shard_map/all_to_all | solution.py:133
  193.0 353.6 %reduce-scatter.2.cloned.1.call-start = ((), (), s32[]{:S(2)}) async-start(), calls=%async_computation.3 | async-start | bytes 2506752 | tf_op jit(solution)/shard_map/reduce_scatter | solution.py:140
  476.3 8.3 %copy-start.4 = (bf16[3,3,3,192]{3,2,1,0:T(4,128)(2,1)S(1)}, bf16[3,3,3,192]{3,2,1,0:T(4,128)(2,1)}, u32[]{:S(2)}) copy-start(bf16[3,3,3,192]{3,2,1,0:T(4,128)(2,1)} %param.17) | copy-start | bytes 31108
  476.3 8.3 %copy-start.3 = (bf16[256,192]{0,1:T(8,128)(2,1)S(1)}, bf16[256,192]{0,1:T(8,128)(2,1)}, u32[]{:S(2)}) copy-start(bf16[256,192]{0,1:T(8,128)(2,1)} %param.15) | copy-start | bytes 294916
  476.6 10.7 %collective-permute-start = (bf16[320,192]{0,1:T(8,128)(2,1)S(1)}, bf16[320,192]{0,1:T(8,128)(2,1)S(1)}, u32[]{:S(2)}, u32[]{:S(2)}) collective-permute-start(bf16[320,192]{0,1:T(8,128)(2,1)S(1)} %copy.36), channel_id=1, source_target_pairs={{0,16},{16,32},{32,48},{48,64},{64,80},{80,96},{96,112},{112,128},... | collective-permute-start | bytes 368648 | tf_op jit(solution)/shard_map/ppermute | solution.py:16
Sparse Core Ops, SparseCore 0:
  10.5 164.0 all-gather.1
  476.5 70.0 reduce-scatter.1
